TPU v7x, 512 devices: a whole 4x4x16 slice. The times are simulated.
512 devices in a mesh: ctx: 64 (over z, y), tp: 8 (over x, core).
Axes of the slice: x: 4, y: 4, z: 16, core: 2. Of those that a mesh axis runs over, the one named last changes fastest.
Arguments:
- features: bfloat16 [3, 4096, 8192], P(None, 'ctx', 'tp'), may hold values from -6 to 6
- short_weight: float32 [3, 3, 8192], P(None, None, 'tp'), may hold values from -3 to 3
- decay_rate: float32 [512, 16], P('tp'), may hold values from 0.00012207031 to 0.03
- residue: float32 [512, 16], P('tp'), may hold values from -3 to 3
- skip_gain: float32 [8192], P('tp'), may hold values from -1 to 1
- out_weight: bfloat16 [8192, 4096], P('tp', 'ctx'), may hold values from -0.1875 to 0.1875
Outputs:
- mixed_out: bfloat16 [4096, 4096], P('ctx', 'tp')
All inputs are finite; a program needn't handle non-finite values.
Results may differ from a plain program's by a relative error of at most 0.006.
Values may be sent and summed in bfloat16 or wider, within the bound.
No kernel may reach another device: no remote copies, remote signals or barrier semaphores. Data moves between devices by JAX's collectives and lax.ppermute only.
A program may use at most 128 MiB of HBM per device.

v0:
```python
import math
import jax
import jax.numpy as jnp
from jax import lax
from jax.sharding import PartitionSpec as P


def passed_along(shard, axis, by):
    length = lax.axis_size(axis)
    pairs = [(i, i + by) for i in range(length) if 0 <= i + by < length]
    return lax.ppermute(shard, axis, pairs)


def entering(value, axis, join, neutral):
    count, mine = (lax.axis_size(axis), lax.axis_index(axis))
    pieces = jax.tree.map(lambda part: lax.all_gather(part, axis), value)
    running = jax.tree.map(
        lambda part, zero: jnp.full_like(part, 0) + jnp.asarray(zero, part.dtype), value, neutral
    )

    def hop(position, running):
        longer = join(running, jax.tree.map(lambda part: part[position], pieces))
        return jax.tree.map(lambda new, old: jnp.where(position < mine, new, old), longer, running)

    return lax.fori_loop(0, count - 1, hop, running)


def combine_states(earlier, later):
    return (earlier[0] * later[0], later[1] + later[0][:, None, :] * earlier[1])


def per_device(features, short_weight, decay_rate, residue, skip_gain, out_weight):
    hi = lax.Precision.HIGHEST
    rows = features.shape[1]
    chans = features.shape[2]
    groups = decay_rate.shape[0]
    modes = decay_rate.shape[1]
    width = chans // groups
    taps = short_weight.shape[1]
    rim = passed_along(features[:, rows - (taps - 1) :, :], "ctx", 1)
    extended = jnp.concatenate([rim, features], axis=1)
    conv = jnp.zeros(features.shape, jnp.float32)
    for j in range(taps):
        conv = conv + short_weight[:, j][:, None, :] * extended[
            :, taps - 1 - j : taps - 1 - j + rows, :
        ].astype(jnp.float32)
    q_lane = conv[0]
    gated = (conv[1] * conv[2]).astype(jnp.bfloat16)
    coef = residue * jnp.sqrt(-jnp.expm1(-2.0 * decay_rate))
    lags = jnp.arange(rows, dtype=jnp.float32)
    near_filter = jnp.sum(
        coef[:, :, None] * jnp.exp(-decay_rate[:, :, None] * lags[None, None, :]), axis=1
    ).astype(jnp.bfloat16)
    index = jnp.arange(rows, dtype=jnp.int32)
    offset = index[:, None] - index[None, :]
    lower = offset >= 0
    clipped = jnp.clip(offset, 0, rows - 1)
    gstep = math.gcd(groups, 8)
    nblock = groups // gstep
    filter_blocks = near_filter.reshape(nblock, gstep, rows)
    input_blocks = gated.reshape(rows, nblock, gstep, width).transpose(1, 0, 2, 3)

    def near_block(pair):
        taps_here, inputs_here = pair
        toeplitz = jnp.where(lower[None], taps_here[:, clipped], jnp.zeros((), jnp.bfloat16))
        return jnp.einsum("gts,sgw->tgw", toeplitz, inputs_here, preferred_element_type=jnp.float32)

    near = (
        lax.map(near_block, (filter_blocks, input_blocks))
        .transpose(1, 0, 2, 3)
        .reshape(rows, chans)
    )
    gated_wide = gated.astype(jnp.float32)
    grouped = gated_wide.reshape(rows, groups, width)
    end_basis = jnp.exp(-decay_rate[None] * (rows - 1.0 - lags)[:, None, None])
    own_state = jnp.einsum("tgs,tgw->gws", end_basis, grouped, precision=hi)
    block_decay = jnp.exp(-decay_rate * rows)
    identity = (
        jnp.ones((groups, modes), jnp.float32),
        jnp.zeros((groups, width, modes), jnp.float32),
    )
    incoming = entering((block_decay, own_state), "ctx", combine_states, identity)[1]
    far_basis = coef[None] * jnp.exp(-decay_rate[None] * (lags + 1.0)[:, None, None])
    far = jnp.einsum("tgs,gws->tgw", far_basis, incoming, precision=hi).reshape(rows, chans)
    mixed = (q_lane * (near + far + skip_gain[None, :] * gated_wide)).astype(jnp.bfloat16)
    partial_out = jnp.dot(
        mixed,
        lax.all_gather(out_weight, "ctx", axis=1, tiled=True),
        preferred_element_type=jnp.float32,
    )
    return lax.psum_scatter(partial_out, "tp", scatter_dimension=1, tiled=True).astype(jnp.bfloat16)


def solution(mesh):
    placed = (
        P(None, "ctx", "tp"),
        P(None, None, "tp"),
        P("tp", None),
        P("tp", None),
        P("tp"),
        P("tp", "ctx"),
    )
    return jax.shard_map(
        per_device, mesh=mesh, in_specs=placed, out_specs=P("ctx", "tp"), check_vma=False
    )
```

profile of v0, /device:TPU:8, one launch (start us, length us, event | category | flops | bytes accessed | tf_op | source)
XLA Modules:
  0.0 521.5 jit_solution(11579085921228791961)
XLA Ops:
  7.4 3.5 collective-permute-start
  12.6 1.4 copy.41
  14.0 2.1 collective-permute-done
  16.5 2.2 multiply_add_fusion
  18.7 1.4 fusion.23
  21.1 113.2 %all-gather.2 = f32[64,64,16]{1,2,0:T(8,128)} all-gather(f32[1,64,16]{1,2,0:T(8,128)S(1)} %get-tuple-element.216), channel_id=3, replica_groups=mesh['ctx'=64,'tp'=8] {'ctx'}, dimensions={0}, use_global_device_ids=true | all-gather | bytes 266240 | tf_op jit(solution)/shard_map/all_gather | solution.py:16
  134.7 108.6 %while.25 = (s32[]{:T(128)}, f32[8,64,8,16]{1,3,2,0:T(8,128)}, bf16[8,64,8,16]{1,3,2,0:T(8,128)(2,1)S(1)}, bf16[8,8,64]{2,1,0:T(8,128)(2,1)S(1)}, s32[]{:T(128)}) while((s32[]{:T(128)}, f32[8,64,8,16]{1,3,2,0:T(8,128)}, bf16[8,64,8,16]{1,3,2,0:T(8,128)(2,1)S(1)}, bf16[8,8,64]{2,1,0:T(8,128)(2,1)S(1)}, s32[]{:T(128)}) %tuple.73), condition=%wide.region_2.3_spmd.clone, body=%wide.region_1.2_spmd.clone.sunk | while | flops 1114114 | bytes 607297 | solution.py:69
  134.9 12.1 %gather_fusion = bf16[4096,8]{1,0:T(8,128)(2,1)S(1)} fusion(bf16[8,64]{0,1:T(8,128)(2,1)S(1)} %bitcast.80, s32[4096]{0:T(1024)S(1)} %broadcast_clamp_fusion.2), kind=kCustom, calls=%fused_computation.clone.clone.1 | custom fusion | bytes 147456 | tf_op jit(solution)/shard_map/while/body/eval_jaxpr/gather | solution.py:65
  148.5 12.1 %gather_fusion = bf16[4096,8]{1,0:T(8,128)(2,1)S(1)} fusion(bf16[8,64]{0,1:T(8,128)(2,1)S(1)} %bitcast.80, s32[4096]{0:T(1024)S(1)} %broadcast_clamp_fusion.2), kind=kCustom, calls=%fused_computation.clone.clone.1 | custom fusion | bytes 147456 | tf_op jit(solution)/shard_map/while/body/eval_jaxpr/gather | solution.py:65
  162.0 12.1 %gather_fusion = bf16[4096,8]{1,0:T(8,128)(2,1)S(1)} fusion(bf16[8,64]{0,1:T(8,128)(2,1)S(1)} %bitcast.80, s32[4096]{0:T(1024)S(1)} %broadcast_clamp_fusion.2), kind=kCustom, calls=%fused_computation.clone.clone.1 | custom fusion | bytes 147456 | tf_op jit(solution)/shard_map/while/body/eval_jaxpr/gather | solution.py:65
  175.6 12.1 %gather_fusion = bf16[4096,8]{1,0:T(8,128)(2,1)S(1)} fusion(bf16[8,64]{0,1:T(8,128)(2,1)S(1)} %bitcast.80, s32[4096]{0:T(1024)S(1)} %broadcast_clamp_fusion.2), kind=kCustom, calls=%fused_computation.clone.clone.1 | custom fusion | bytes 147456 | tf_op jit(solution)/shard_map/while/body/eval_jaxpr/gather | solution.py:65
  189.2 12.1 %gather_fusion = bf16[4096,8]{1,0:T(8,128)(2,1)S(1)} fusion(bf16[8,64]{0,1:T(8,128)(2,1)S(1)} %bitcast.80, s32[4096]{0:T(1024)S(1)} %broadcast_clamp_fusion.2), kind=kCustom, calls=%fused_computation.clone.clone.1 | custom fusion | bytes 147456 | tf_op jit(solution)/shard_map/while/body/eval_jaxpr/gather | solution.py:65
  202.8 12.1 %gather_fusion = bf16[4096,8]{1,0:T(8,128)(2,1)S(1)} fusion(bf16[8,64]{0,1:T(8,128)(2,1)S(1)} %bitcast.80, s32[4096]{0:T(1024)S(1)} %broadcast_clamp_fusion.2), kind=kCustom, calls=%fused_computation.clone.clone.1 | custom fusion | bytes 147456 | tf_op jit(solution)/shard_map/while/body/eval_jaxpr/gather | solution.py:65
  216.3 12.1 %gather_fusion = bf16[4096,8]{1,0:T(8,128)(2,1)S(1)} fusion(bf16[8,64]{0,1:T(8,128)(2,1)S(1)} %bitcast.80, s32[4096]{0:T(1024)S(1)} %broadcast_clamp_fusion.2), kind=kCustom, calls=%fused_computation.clone.clone.1 | custom fusion | bytes 147456 | tf_op jit(solution)/shard_map/while/body/eval_jaxpr/gather | solution.py:65
  229.9 12.1 %gather_fusion = bf16[4096,8]{1,0:T(8,128)(2,1)S(1)} fusion(bf16[8,64]{0,1:T(8,128)(2,1)S(1)} %bitcast.80, s32[4096]{0:T(1024)S(1)} %broadcast_clamp_fusion.2), kind=kCustom, calls=%fused_computation.clone.clone.1 | custom fusion | bytes 147456 | tf_op jit(solution)/shard_map/while/body/eval_jaxpr/gather | solution.py:65
  243.3 71.3 %all-gather.8.cloned.1.call-done = f32[4096,16,16]{2,1,0:T(8,128)} async-done(((f32[64,16,16]{2,1,0:T(8,128)}), f32[4096,16,16]{2,1,0:T(8,128)}) %all-gather.8.cloned.1.call-update) | async-done | bytes 4194320 | tf_op jit(solution)/shard_map/all_gather | solution.py:16
  314.6 22.6 %copy.48 = f32[64,64,16,16]{1,3,2,0:T(8,128)} copy(f32[64,64,16,16]{3,2,1,0:T(8,128)} %bitcast.81) | data formatting | bytes 8388608
  337.2 106.0 %while.26 = (s32[]{:T(128)}, f32[64,16,16]{0,2,1:T(8,128)S(1)}, s32[]{:T(128)}, f32[64,64,16,16]{1,3,2,0:T(8,128)}, f32[64,64,16]{1,2,0:T(8,128)}, /*index=5*/s32[]{:T(128)}, s32[]{:T(128)}) while((s32[]{:T(128)}, f32[64,16,16]{0,2,1:T(8,128)S(1)}, s32[]{:T(128)}, f32[64,64,16,16]{1,3,2,0:T(8,128)}, f32[64,64,16]{1,2,0:T(8,128)}, ...), condition=%wide.region_4.5_spmd.clone, body=%wide.region_3.4_spmd.clone.sunk | while | flops 65540 | bytes 209001 | solution.py:25
  338.0 1.0 fusion.46
  401.8 1.0 fusion.46
  408.6 1.0 fusion.46
  410.2 1.0 fusion.46
  413.6 1.0 fusion.46
  422.0 1.0 fusion.46
  427.1 1.0 fusion.46
  430.4 1.0 fusion.46
  432.1 1.0 fusion.46
  433.8 1.0 fusion.46
  444.5 25.6 %all-gather.6.cloned.1.call-done = bf16[1024,4096]{0,1:T(8,128)(2,1)} async-done(((bf16[1024,64]{0,1:T(8,128)(2,1)}), bf16[1024,4096]{0,1:T(8,128)(2,1)}) %all-gather.6.cloned.1.call-update) | async-done | bytes 8388624 | tf_op jit(solution)/shard_map/all_gather | solution.py:88
  470.1 7.0 %fusion.32 = f32[64,4096]{1,0:T(8,128)} fusion(bf16[64,1024]{0,1:T(8,128)(2,1)S(1)} %fusion.17, bf16[1024,4096]{0,1:T(8,128)(2,1)} %all-gather.6.cloned.1.call-done), kind=kOutput, calls=%fused_computation.53 | convolution fusion | flops 536870912 | bytes 9568256 | tf_op jit(solution)/shard_map/dot_general | solution.py:86
  477.2 36.2 %reduce-scatter.2.cloned.1.call-done = f32[64,512]{1,0:T(8,128)} async-done(((f32[64,4096]{1,0:T(8,128)}), f32[64,512]{1,0:T(8,128)}) %reduce-scatter.2.cloned.1.call-update) | async-done | bytes 131088 | tf_op jit(solution)/shard_map/reduce_scatter | solution.py:91
  513.4 1.5 convert_element_type.51
  (207 shorter events, 112.3 us)
Async XLA Ops:
  6.5 308.0 %all-gather.8.cloned.1.call-start = ((), (), s32[]{:S(2)}) async-start(), calls=%async_computation.3 | async-start | bytes 34078720 | tf_op jit(solution)/shard_map/all_gather | solution.py:16
  7.4 8.7 %collective-permute-start = (bf16[3,2,1024]{2,1,0:T(2,128)(2,1)S(1)}, bf16[3,2,1024]{2,1,0:T(2,128)(2,1)S(1)}, u32[]{:S(2)}, u32[]{:S(2)}) collective-permute-start(bf16[3,2,1024]{2,1,0:T(2,128)(2,1)S(1)} %slice.29), channel_id=1, source_target_pairs={{0,8},{8,16},{16,24},{24,32},{32,40},{40,48},{48,56},{56,64},{64,7... | collective-permute-start | bytes 36872 | tf_op jit(solution)/shard_map/ppermute | solution.py:11
  20.2 449.9 %all-gather.6.cloned.1.call-start = ((), (), s32[]{:S(2)}) async-start(), calls=%async_computation.1 | async-start | bytes 8519680 | tf_op jit(solution)/shard_map/all_gather | solution.py:88
  21.0 492.4 %reduce-scatter.2.cloned.1.call-start = ((), (), s32[]{:S(2)}) async-start(), calls=%async_computation.2 | async-start | bytes 1179648 | tf_op jit(solution)/shard_map/reduce_scatter | solution.py:91
  337.2 107.1 %copy-start = (f32[8,64,8,16]{1,3,2,0:T(8,128)S(1)}, f32[8,64,8,16]{1,3,2,0:T(8,128)}, u32[]{:S(2)}) copy-start(f32[8,64,8,16]{1,3,2,0:T(8,128)} %get-tuple-element.131) | copy-start | bytes 786436
  337.2 107.1 %copy-start.1 = (f32[1024]{0:T(1024)S(1)}, f32[1024]{0:T(1024)}, u32[]{:S(2)}) copy-start(f32[1024]{0:T(1024)} %param.14) | copy-start | bytes 12292
Sparse Core Ops, SparseCore 0:
  20.3 294.1 all-gather.7
  317.5 152.5 all-gather.5
  477.3 36.0 reduce-scatter.1
where the time goes:
time: 526 us; the launch traced here: 521 us
  local copies, waits for them, and re-layouts  173 us (33%)
  waiting for transfers between devices  136 us (26%)
  blocking collectives  113 us (21%)
  other arithmetic  65.9 us (13%)
  matrix products  15.8 us (3%)
  between operations  13.2 us (3%)
    all_gather x1, blocking collectives, entering(): pieces = jax.tree.map(lambda part: lax.all_gather(part, axis), value)  113 us
    gather x16, local copies, waits for them, and re-layouts, near_block(): taps_here[:, clipped]  100 us
    all_gather x1, waiting for transfers between devices, entering(): pieces = jax.tree.map(lambda part: lax.all_gather(part, axis), value)  71.3 us
    select_n x63, other arithmetic, hop(): jnp.where(position < mine, new, old)  60.5 us
    mul x63, local copies, waits for them, and re-layouts, combine_states(): return (earlier[0] * later[0], later[1] + later[0][:, None, :] * earlier[1])  44.3 us
    reduce_scatter x1, waiting for transfers between devices, per_device(): lax.psum_scatter(partial_out, 'tp', scatter_dimension=1, tiled=True)  36.2 us
    all_gather x1, waiting for transfers between devices, per_device(): lax.all_gather(out_weight, 'ctx', axis=1, tiled=True)  25.6 us
    unnamed x8, local copies, waits for them, and re-layouts  24 us
  transfers between devices with their start and end apart: 4, of which 4 were waited for; matrix products, arithmetic and copies ran while one was open for 46% of the time, Pallas kernels for 0%

commit v1 on v0

--- a/solution.py
+++ b/solution.py
@@ -85,7 +85,9 @@
     mixed = (q_lane * (near + far + skip_gain[None, :] * gated_wide)).astype(jnp.bfloat16)
     partial_out = jnp.dot(
         mixed,
-        lax.all_gather(out_weight, "ctx", axis=1, tiled=True),
+        jnp.concatenate(
+            lax.all_to_all(jnp.stack([out_weight] * lax.axis_size("ctx")), "ctx", 0, 0), axis=1
+        ),
         preferred_element_type=jnp.float32,
     )
     return lax.psum_scatter(partial_out, "tp", scatter_dimension=1, tiled=True).astype(jnp.bfloat16)

time: 526 us -> 875 us (1.66)
  blocking collectives: 113 us -> 463 us
  waiting for transfers between devices: 136 us -> 114 us
  starting transfers between devices: 3.57 us -> 22.5 us
    all_gather x1, blocking collectives: 113 us -> 463 us  [entering(): pieces = jax.tree.map(lambda part: lax.all_gather(part, axis), value)]
    all_gather x1 -> x0, waiting for transfers between devices: 25.6 us -> none  [per_device(): lax.all_gather(out_weight, 'ctx', axis=1, tiled=True)]
    all_to_all x0 -> x1, starting transfers between devices: none -> 19.1 us  [per_device(): lax.all_to_all(jnp.stack([out_weight] * lax.axis_size('ctx')), 'ctx', 0, 0)]
    unnamed x8 -> x16, local copies, waits for them, and re-layouts: 24 us -> 23 us
  transfers between devices with their start and end apart: 4 -> 4, of which waited for: 4 -> 3; matrix products, arithmetic and copies ran while one was open for 46% -> 28% of each run, Pallas kernels for 0% -> 0%
where the time goes in v1:
time: 875 us; the launch traced here: 871 us
  blocking collectives  463 us (53%)
  local copies, waits for them, and re-layouts  175 us (20%)
  waiting for transfers between devices  114 us (13%)
  other arithmetic  65.1 us (7%)
  starting transfers between devices  22.5 us (3%)
  matrix products  15.8 us (2%)
  between operations  13.6 us (2%)
    all_gather x1, blocking collectives, entering(): pieces = jax.tree.map(lambda part: lax.all_gather(part, axis), value)  463 us
    gather x16, local copies, waits for them, and re-layouts, near_block(): taps_here[:, clipped]  100 us
    all_gather x1, waiting for transfers between devices, entering(): pieces = jax.tree.map(lambda part: lax.all_gather(part, axis), value)  72.6 us
    select_n x63, other arithmetic, hop(): jnp.where(position < mine, new, old)  60.4 us
    mul x63, local copies, waits for them, and re-layouts, combine_states(): return (earlier[0] * later[0], later[1] + later[0][:, None, :] * earlier[1])  44.3 us
    reduce_scatter x1, waiting for transfers between devices, per_device(): lax.psum_scatter(partial_out, 'tp', scatter_dimension=1, tiled=True)  37.6 us
    unnamed x16, local copies, waits for them, and re-layouts  23 us
    all_to_all x1, starting transfers between devices, per_device(): lax.all_to_all(jnp.stack([out_weight] * lax.axis_size('ctx')), 'ctx', 0, 0)  19.1 us
  transfers between devices with their start and end apart: 4, of which 3 were waited for; matrix products, arithmetic and copies ran while one was open for 28% of the time, Pallas kernels for 0%

profile of v1, /device:TPU:8, one launch (start us, length us, event | category | flops | bytes accessed | tf_op | source)
XLA Modules:
  0.0 870.7 jit_solution(16698755845882060446)
XLA Ops:
  6.5 5.2 stack.2
  11.7 19.1 %all-to-all-start = ((bf16[64,1024,64]{1,2,0:T(8,128)(2,1)}), bf16[64,1024,64]{1,2,0:T(8,128)(2,1)}, u32[]{:S(2)}, u32[]{:S(2)}) async-start(bf16[64,1024,64]{1,2,0:T(8,128)(2,1)} %stack.2), calls=%async_computation | async-start | bytes 16777216 | tf_op jit(solution)/shard_map/all_to_all | solution.py:89
  30.9 3.4 collective-permute-start
  34.9 3.6 collective-permute-done
  38.9 2.2 multiply_add_fusion
  41.1 1.4 fusion.22
  42.8 463.4 %all-gather.2 = f32[64,64,16]{1,2,0:T(8,128)} all-gather(f32[1,64,16]{1,2,0:T(8,128)S(1)} %get-tuple-element.215), channel_id=3, replica_groups=mesh['ctx'=64,'tp'=8] {'ctx'}, dimensions={0}, use_global_device_ids=true | all-gather | bytes 266240 | tf_op jit(solution)/shard_map/all_gather | solution.py:16
  506.6 108.6 %while.25 = (s32[]{:T(128)}, f32[8,64,8,16]{1,3,2,0:T(8,128)}, bf16[8,64,8,16]{1,3,2,0:T(8,128)(2,1)S(1)}, bf16[8,8,64]{2,1,0:T(8,128)(2,1)S(1)}, s32[]{:T(128)}) while((s32[]{:T(128)}, f32[8,64,8,16]{1,3,2,0:T(8,128)}, bf16[8,64,8,16]{1,3,2,0:T(8,128)(2,1)S(1)}, bf16[8,8,64]{2,1,0:T(8,128)(2,1)S(1)}, s32[]{:T(128)}) %tuple.71), condition=%wide.region_2.3_spmd.clone, body=%wide.region_1.2_spmd.clone.sunk | while | flops 1114114 | bytes 607297 | solution.py:69
  506.8 12.1 %gather_fusion = bf16[4096,8]{1,0:T(8,128)(2,1)S(1)} fusion(bf16[8,64]{0,1:T(8,128)(2,1)S(1)} %bitcast.77, s32[4096]{0:T(1024)S(1)} %broadcast_clamp_fusion.2), kind=kCustom, calls=%fused_computation.clone.clone.1 | custom fusion | bytes 147456 | tf_op jit(solution)/shard_map/while/body/eval_jaxpr/gather | solution.py:65
  520.4 12.1 %gather_fusion = bf16[4096,8]{1,0:T(8,128)(2,1)S(1)} fusion(bf16[8,64]{0,1:T(8,128)(2,1)S(1)} %bitcast.77, s32[4096]{0:T(1024)S(1)} %broadcast_clamp_fusion.2), kind=kCustom, calls=%fused_computation.clone.clone.1 | custom fusion | bytes 147456 | tf_op jit(solution)/shard_map/while/body/eval_jaxpr/gather | solution.py:65
  534.0 12.1 %gather_fusion = bf16[4096,8]{1,0:T(8,128)(2,1)S(1)} fusion(bf16[8,64]{0,1:T(8,128)(2,1)S(1)} %bitcast.77, s32[4096]{0:T(1024)S(1)} %broadcast_clamp_fusion.2), kind=kCustom, calls=%fused_computation.clone.clone.1 | custom fusion | bytes 147456 | tf_op jit(solution)/shard_map/while/body/eval_jaxpr/gather | solution.py:65
  547.5 12.1 %gather_fusion = bf16[4096,8]{1,0:T(8,128)(2,1)S(1)} fusion(bf16[8,64]{0,1:T(8,128)(2,1)S(1)} %bitcast.77, s32[4096]{0:T(1024)S(1)} %broadcast_clamp_fusion.2), kind=kCustom, calls=%fused_computation.clone.clone.1 | custom fusion | bytes 147456 | tf_op jit(solution)/shard_map/while/body/eval_jaxpr/gather | solution.py:65
  561.1 12.1 %gather_fusion = bf16[4096,8]{1,0:T(8,128)(2,1)S(1)} fusion(bf16[8,64]{0,1:T(8,128)(2,1)S(1)} %bitcast.77, s32[4096]{0:T(1024)S(1)} %broadcast_clamp_fusion.2), kind=kCustom, calls=%fused_computation.clone.clone.1 | custom fusion | bytes 147456 | tf_op jit(solution)/shard_map/while/body/eval_jaxpr/gather | solution.py:65
  574.7 12.1 %gather_fusion = bf16[4096,8]{1,0:T(8,128)(2,1)S(1)} fusion(bf16[8,64]{0,1:T(8,128)(2,1)S(1)} %bitcast.77, s32[4096]{0:T(1024)S(1)} %broadcast_clamp_fusion.2), kind=kCustom, calls=%fused_computation.clone.clone.1 | custom fusion | bytes 147456 | tf_op jit(solution)/shard_map/while/body/eval_jaxpr/gather | solution.py:65
  588.3 12.1 %gather_fusion = bf16[4096,8]{1,0:T(8,128)(2,1)S(1)} fusion(bf16[8,64]{0,1:T(8,128)(2,1)S(1)} %bitcast.77, s32[4096]{0:T(1024)S(1)} %broadcast_clamp_fusion.2), kind=kCustom, calls=%fused_computation.clone.clone.1 | custom fusion | bytes 147456 | tf_op jit(solution)/shard_map/while/body/eval_jaxpr/gather | solution.py:65
  601.8 12.1 %gather_fusion = bf16[4096,8]{1,0:T(8,128)(2,1)S(1)} fusion(bf16[8,64]{0,1:T(8,128)(2,1)S(1)} %bitcast.77, s32[4096]{0:T(1024)S(1)} %broadcast_clamp_fusion.2), kind=kCustom, calls=%fused_computation.clone.clone.1 | custom fusion | bytes 147456 | tf_op jit(solution)/shard_map/while/body/eval_jaxpr/gather | solution.py:65
  615.2 72.6 %all-gather.5.cloned.1.call-done = f32[4096,16,16]{2,1,0:T(8,128)} async-done(((f32[64,16,16]{2,1,0:T(8,128)}), f32[4096,16,16]{2,1,0:T(8,128)}) %all-gather.5.cloned.1.call-update) | async-done | bytes 4194320 | tf_op jit(solution)/shard_map/all_gather | solution.py:16
  687.8 22.6 %copy.49 = f32[64,64,16,16]{1,3,2,0:T(8,128)} copy(f32[64,64,16,16]{3,2,1,0:T(8,128)} %bitcast.78) | data formatting | bytes 8388608
  710.4 105.8 %while.26 = (s32[]{:T(128)}, f32[64,16,16]{0,2,1:T(8,128)S(1)}, s32[]{:T(128)}, f32[64,64,16,16]{1,3,2,0:T(8,128)}, f32[64,64,16]{1,2,0:T(8,128)}, /*index=5*/s32[]{:T(128)}, s32[]{:T(128)}) while((s32[]{:T(128)}, f32[64,16,16]{0,2,1:T(8,128)S(1)}, s32[]{:T(128)}, f32[64,64,16,16]{1,3,2,0:T(8,128)}, f32[64,64,16]{1,2,0:T(8,128)}, ...), condition=%wide.region_4.5_spmd.clone, body=%wide.region_3.4_spmd.clone.sunk | while | flops 65540 | bytes 209001 | solution.py:25
  711.2 1.0 fusion.45
  714.5 1.0 fusion.45
  716.2 1.0 fusion.45
  719.6 1.0 fusion.45
  721.2 1.0 fusion.45
  724.6 1.0 fusion.45
  726.3 1.0 fusion.45
  728.0 1.0 fusion.45
  731.3 1.0 fusion.45
  733.0 1.0 fusion.45
  817.6 7.0 fusion.25
  824.7 37.6 %reduce-scatter.2.cloned.1.call-done = f32[64,512]{1,0:T(8,128)} async-done(((f32[64,4096]{1,0:T(8,128)}), f32[64,512]{1,0:T(8,128)}) %reduce-scatter.2.cloned.1.call-update) | async-done | bytes 131088 | tf_op jit(solution)/shard_map/reduce_scatter | solution.py:93
  862.4 1.5 convert_element_type.52
  (215 shorter events, 109.6 us)
Async XLA Ops:
  11.7 19.1 %copy-start.1 = (bf16[3,64,1024]{2,1,0:T(8,128)(2,1)S(1)}, bf16[3,64,1024]{2,1,0:T(8,128)(2,1)}, u32[]{:S(2)}) copy-start(bf16[3,64,1024]{2,1,0:T(8,128)(2,1)} %param.10) | copy-start | bytes 1179652
  11.7 22.5 %copy-start.3 = (f32[64,16]{0,1:T(8,128)S(1)}, f32[64,16]{0,1:T(8,128)}, u32[]{:S(2)}) copy-start(f32[64,16]{0,1:T(8,128)} %param.12) | copy-start | bytes 12292
  11.7 22.5 %copy-start.4 = (f32[64,16]{0,1:T(8,128)S(1)}, f32[64,16]{0,1:T(8,128)}, u32[]{:S(2)}) copy-start(f32[64,16]{0,1:T(8,128)} %param.13) | copy-start | bytes 12292
  11.7 22.6 %copy-start.2 = (f32[3,3,1024]{2,1,0:T(4,128)S(1)}, f32[3,3,1024]{2,1,0:T(4,128)}, u32[]{:S(2)}) copy-start(f32[3,3,1024]{2,1,0:T(4,128)} %param.11) | copy-start | bytes 110596
  11.7 805.9 %all-to-all-start = ((bf16[64,1024,64]{1,2,0:T(8,128)(2,1)}), bf16[64,1024,64]{1,2,0:T(8,128)(2,1)}, u32[]{:S(2)}, u32[]{:S(2)}) async-start(bf16[64,1024,64]{1,2,0:T(8,128)(2,1)} %stack.2), calls=%async_computation | async-start | bytes 16777216 | tf_op jit(solution)/shard_map/all_to_all | solution.py:89
  30.8 657.0 %all-gather.5.cloned.1.call-start = ((), (), s32[]{:S(2)}) async-start(), calls=%async_computation.3 | async-start | bytes 34078720 | tf_op jit(solution)/shard_map/all_gather | solution.py:16
  30.9 7.6 collective-permute-start
  42.6 819.8 %reduce-scatter.2.cloned.1.call-start = ((), (), s32[]{:S(2)}) async-start(), calls=%async_computation.2 | async-start | bytes 1179648 | tf_op jit(solution)/shard_map/reduce_scatter | solution.py:93
  710.4 107.0 %copy-start = (f32[8,64,8,16]{1,3,2,0:T(8,128)S(1)}, f32[8,64,8,16]{1,3,2,0:T(8,128)}, u32[]{:S(2)}) copy-start(f32[8,64,8,16]{1,3,2,0:T(8,128)} %get-tuple-element.131) | copy-start | bytes 786436
  710.4 107.0 %copy-start.5 = (f32[1024]{0:T(1024)S(1)}, f32[1024]{0:T(1024)}, u32[]{:S(2)}) copy-start(f32[1024]{0:T(1024)} %param.14) | copy-start | bytes 12292
Sparse Core Ops, SparseCore 0:
  42.7 645.0 all-gather.4
  824.8 37.4 reduce-scatter.1
